TPU v7x, 256 devices: a whole 4x4x8 slice. The times are simulated.
256 devices in a mesh: section: 16 (over z_lo, x, core), tp: 16 (over y, z_hi).
Axes of the slice: x: 4, y: 4, z: 8 (z_hi: 4, z_lo: 2; z = z_hi * 2 + z_lo), core: 2. Of those that a mesh axis runs over, the one named last changes fastest.
Arguments:
- tokens: bfloat16 [2, 512, 4096], P(None, 'tp'), may hold values from -6 to 6
- norm_gains: float32 [2, 4096], replicated, may hold values from 0.1 to 1.9
- w_gate: bfloat16 [16, 4096, 2048], P('section', None, 'tp'), may hold values from -0.09375 to 0.09375
- w_up: bfloat16 [16, 4096, 2048], P('section', None, 'tp'), may hold values from -0.09375 to 0.09375
- w_down: bfloat16 [16, 2048, 4096], P('section', 'tp'), may hold values from -0.0625 to 0.0625
Outputs:
- acts: bfloat16 [16, 2, 512, 512], P('section', None, 'tp')
All inputs are finite; a program needn't handle non-finite values.
Results may differ from a plain program's by a relative error of at most 0.022.
Values may be sent and summed in bfloat16 or wider, within the bound.
No kernel may reach another device: no remote copies, remote signals or barrier semaphores. Data moves between devices by JAX's collectives and lax.ppermute only.
A program may use at most 64 MiB of HBM per device.

v0:
```python
import jax
import jax.numpy as jnp
from jax import lax
from jax.sharding import PartitionSpec as P

LAYERS = 2


epsilon = 1e-05


def swapped(value, axis, stride):
    mask = 2**stride
    pairs = [(source, source ^ mask) for source in range(lax.axis_size(axis))]
    return lax.ppermute(value, axis, pairs)


def shifted(value, axis, steps):
    count = lax.axis_size(axis)
    leading, last = (max(0, -steps), min(count, count - steps))
    return lax.ppermute(value, axis, [(source, source + steps) for source in range(leading, last)])


def body(tokens, norm_gains, w_gate, w_up, w_down):
    section_count = lax.axis_size("section")
    split = section_count // LAYERS
    bit_count = split.bit_length() - 1
    position = lax.axis_index("section")
    section_layer = position // split
    member = position % split
    gate_local = w_gate[0]
    up_local = w_up[0]
    down_local = w_down[0]
    norm_gain = lax.dynamic_index_in_dim(norm_gains, section_layer, 0, keepdims=False)
    micro_count, tok_dev, model_width = tokens.shape
    piece_width = model_width // split
    pieces = 1
    piece_count = micro_count * pieces
    row_count = tok_dev // pieces
    tick_count = piece_count + LAYERS - 1

    def project(row_block):
        gate_proj = jnp.dot(row_block, gate_local, preferred_element_type=jnp.float32)
        up_proj = jnp.dot(row_block, up_local, preferred_element_type=jnp.float32)
        active = (jax.nn.silu(gate_proj) * up_proj).astype(jnp.bfloat16)
        return jnp.dot(active, down_local, preferred_element_type=jnp.float32)

    def partial_sum(incoming):
        current = incoming.astype(jnp.float32)
        inv_rms = lax.rsqrt(jnp.mean(current * current, axis=1, keepdims=True) + epsilon)
        normed = (current * inv_rms * norm_gain).astype(jnp.bfloat16)
        row_terms = project(lax.all_gather(normed, "tp", axis=0, tiled=True))
        return (
            current,
            lax.psum_scatter(
                row_terms.astype(jnp.bfloat16), "tp", scatter_dimension=0, tiled=True
            ).astype(jnp.float32),
        )

    def advance(tick_index, tick_state):
        received, stored = tick_state
        micro_index = tick_index - section_layer
        in_window = (micro_index >= 0) & (micro_index < piece_count)
        store_slot = jnp.clip(micro_index, 0, piece_count - 1)
        first_input = lax.dynamic_index_in_dim(
            tokens, jnp.clip(tick_index, 0, piece_count - 1), 0, keepdims=False
        )
        incoming = jnp.where(section_layer == 0, first_input, received)
        current, partial_value = partial_sum(incoming)
        summed = partial_value
        for level in range(bit_count):
            summed = summed + swapped(summed.astype(jnp.bfloat16), "section", level).astype(
                summed.dtype
            )
        full_result = (current + summed).astype(jnp.bfloat16)
        result = lax.dynamic_slice_in_dim(full_result, member * piece_width, piece_width, 1)
        forward = shifted(full_result, "section", split)
        previous = lax.dynamic_index_in_dim(stored, store_slot, 0, keepdims=False)
        stored = lax.dynamic_update_index_in_dim(
            stored, jnp.where(in_window, result, previous), store_slot, 0
        )
        return (forward, stored)

    start_rows = jnp.zeros((row_count, model_width), jnp.bfloat16)
    start_store = jnp.zeros((piece_count, row_count, piece_width), jnp.bfloat16)
    final_rows, stored = lax.fori_loop(0, tick_count, advance, (start_rows, start_store))
    return stored.reshape(1, micro_count, tok_dev, piece_width)


def solution(mesh):
    in_specs = (
        P(None, "tp", None),
        P(),
        P("section", None, "tp"),
        P("section", None, "tp"),
        P("section", "tp", None),
    )
    out_specs = P("section", None, "tp", None)
    return jax.shard_map(body, mesh=mesh, in_specs=in_specs, out_specs=out_specs, check_vma=False)
```

profile of v0, /device:TPU:32, one launch (start us, length us, event | category | flops | bytes accessed | tf_op | source)
XLA Modules:
  0.0 668.1 jit_solution(9687036157955417888)
XLA Ops:
  7.4 653.3 %while.17 = (s32[]{:T(128)}, bf16[32,4096]{1,0:T(8,128)(2,1)S(1)}, bf16[2,32,512]{2,1,0:T(8,128)(2,1)S(1)}, pred[]{:T(512)}, bf16[2,32,4096]{2,1,0:T(8,128)(2,1)...) while((s32[]{:T(128)}, bf16[32,4096]{1,0:T(8,128)(2,1)S(1)}, ...), condition=%wide.region_3.4_spmd, body=%wide.region_0.3_spmd.sunk | while | flops 1616789504 | bytes 60474380 | solution.py:86
  9.7 80.3 %all-gather.2.cloned.1.call-done = bf16[512,4096]{1,0:T(8,128)(2,1)} async-done(((bf16[32,4096]{1,0:T(8,128)(2,1)}), bf16[512,4096]{1,0:T(8,128)(2,1)}) %all-gather.2.cloned.1.call-update) | async-done | bytes 4194320 | tf_op jit(solution)/shard_map/while/body/eval_jaxpr/all_gather | solution.py:52
  89.9 3.7 fusion.38
  93.7 8.6 %convolution_convert_fusion.2 = bf16[512,4096]{1,0:T(8,128)(2,1)} fusion(bf16[128,4096]{1,0:T(8,128)(2,1)S(1)} %copy-done.2, bf16[512,4096]{1,0:T(8,128)(2,1)} %all-gather.2.cloned.1.call-done, bf16[4096,128]{1,0:T(8,128)(2,1)S(1)} %copy-done.1, f32[512,128]{1,0:T(8,128)S(1)} %fusion.38), kind=kOutput, calls=%fused_computation.clone.1 | convolution fusion | flops 1076232192 | bytes 10747904 | tf_op jit(solution)/shard_map/while/body/eval_jaxpr/dot_general | solution.py:46
  102.3 94.2 %reduce-scatter.2.cloned.1.call-done = bf16[32,4096]{1,0:T(8,128)(2,1)} async-done(((bf16[512,4096]{1,0:T(8,128)(2,1)}), bf16[32,4096]{1,0:T(8,128)(2,1)}) %reduce-scatter.2.cloned.1.call-update) | async-done | bytes 262160 | tf_op jit(solution)/shard_map/while/body/eval_jaxpr/reduce_scatter | solution.py:55
  196.6 1.7 collective-permute-done
  199.3 1.5 collective-permute-start.1
  200.8 6.9 %collective-permute-done.1 = bf16[32,4096]{1,0:T(8,128)(2,1)S(1)} collective-permute-done((bf16[32,4096]{1,0:T(8,128)(2,1)S(1)}, bf16[32,4096]{1,0:T(8,128)(2,1)S(1)}, u32[]{:S(2)}, u32[]{:S(2)}) %collective-permute-start.1) | collective-permute-done | bytes 262176 | tf_op jit(solution)/shard_map/while/body/eval_jaxpr/ppermute | solution.py:15
  208.8 3.1 collective-permute-start.2
  211.9 6.0 collective-permute-done.2
  220.4 7.2 %collective-permute-done.3 = bf16[32,4096]{1,0:T(8,128)(2,1)S(1)} collective-permute-done((bf16[32,4096]{1,0:T(8,128)(2,1)S(1)}, bf16[32,4096]{1,0:T(8,128)(2,1)S(1)}, u32[]{:S(2)}, u32[]{:S(2)}) %collective-permute-start.3) | collective-permute-done | bytes 262176 | tf_op jit(solution)/shard_map/while/body/eval_jaxpr/ppermute | solution.py:21
  229.8 76.5 %all-gather.2.cloned.1.call-done = bf16[512,4096]{1,0:T(8,128)(2,1)} async-done(((bf16[32,4096]{1,0:T(8,128)(2,1)}), bf16[512,4096]{1,0:T(8,128)(2,1)}) %all-gather.2.cloned.1.call-update) | async-done | bytes 4194320 | tf_op jit(solution)/shard_map/while/body/eval_jaxpr/all_gather | solution.py:52
  306.3 3.7 fusion.38
  310.0 8.6 %convolution_convert_fusion.2 = bf16[512,4096]{1,0:T(8,128)(2,1)} fusion(bf16[128,4096]{1,0:T(8,128)(2,1)S(1)} %copy-done.2, bf16[512,4096]{1,0:T(8,128)(2,1)} %all-gather.2.cloned.1.call-done, bf16[4096,128]{1,0:T(8,128)(2,1)S(1)} %copy-done.1, f32[512,128]{1,0:T(8,128)S(1)} %fusion.38), kind=kOutput, calls=%fused_computation.clone.1 | convolution fusion | flops 1076232192 | bytes 10747904 | tf_op jit(solution)/shard_map/while/body/eval_jaxpr/dot_general | solution.py:46
  318.7 94.4 %reduce-scatter.2.cloned.1.call-done = bf16[32,4096]{1,0:T(8,128)(2,1)} async-done(((bf16[512,4096]{1,0:T(8,128)(2,1)}), bf16[32,4096]{1,0:T(8,128)(2,1)}) %reduce-scatter.2.cloned.1.call-update) | async-done | bytes 262160 | tf_op jit(solution)/shard_map/while/body/eval_jaxpr/reduce_scatter | solution.py:55
  413.0 1.7 collective-permute-done
  415.8 1.6 collective-permute-start.1
  417.4 6.9 %collective-permute-done.1 = bf16[32,4096]{1,0:T(8,128)(2,1)S(1)} collective-permute-done((bf16[32,4096]{1,0:T(8,128)(2,1)S(1)}, bf16[32,4096]{1,0:T(8,128)(2,1)S(1)}, u32[]{:S(2)}, u32[]{:S(2)}) %collective-permute-start.1) | collective-permute-done | bytes 262176 | tf_op jit(solution)/shard_map/while/body/eval_jaxpr/ppermute | solution.py:15
  425.3 3.1 collective-permute-start.2
  428.4 6.0 collective-permute-done.2
  436.8 7.2 %collective-permute-done.3 = bf16[32,4096]{1,0:T(8,128)(2,1)S(1)} collective-permute-done((bf16[32,4096]{1,0:T(8,128)(2,1)S(1)}, bf16[32,4096]{1,0:T(8,128)(2,1)S(1)}, u32[]{:S(2)}, u32[]{:S(2)}) %collective-permute-start.3) | collective-permute-done | bytes 262176 | tf_op jit(solution)/shard_map/while/body/eval_jaxpr/ppermute | solution.py:21
  444.0 1.3 fusion.36
  446.3 76.2 %all-gather.2.cloned.1.call-done = bf16[512,4096]{1,0:T(8,128)(2,1)} async-done(((bf16[32,4096]{1,0:T(8,128)(2,1)}), bf16[512,4096]{1,0:T(8,128)(2,1)}) %all-gather.2.cloned.1.call-update) | async-done | bytes 4194320 | tf_op jit(solution)/shard_map/while/body/eval_jaxpr/all_gather | solution.py:52
  522.5 3.7 fusion.38
  526.2 8.6 %convolution_convert_fusion.2 = bf16[512,4096]{1,0:T(8,128)(2,1)} fusion(bf16[128,4096]{1,0:T(8,128)(2,1)S(1)} %copy-done.2, bf16[512,4096]{1,0:T(8,128)(2,1)} %all-gather.2.cloned.1.call-done, bf16[4096,128]{1,0:T(8,128)(2,1)S(1)} %copy-done.1, f32[512,128]{1,0:T(8,128)S(1)} %fusion.38), kind=kOutput, calls=%fused_computation.clone.1 | convolution fusion | flops 1076232192 | bytes 10747904 | tf_op jit(solution)/shard_map/while/body/eval_jaxpr/dot_general | solution.py:46
  534.9 94.8 %reduce-scatter.2.cloned.1.call-done = bf16[32,4096]{1,0:T(8,128)(2,1)} async-done(((bf16[512,4096]{1,0:T(8,128)(2,1)}), bf16[32,4096]{1,0:T(8,128)(2,1)}) %reduce-scatter.2.cloned.1.call-update) | async-done | bytes 262160 | tf_op jit(solution)/shard_map/while/body/eval_jaxpr/reduce_scatter | solution.py:55
  629.7 1.7 collective-permute-done
  632.4 1.5 collective-permute-start.1
  634.0 6.9 %collective-permute-done.1 = bf16[32,4096]{1,0:T(8,128)(2,1)S(1)} collective-permute-done((bf16[32,4096]{1,0:T(8,128)(2,1)S(1)}, bf16[32,4096]{1,0:T(8,128)(2,1)S(1)}, u32[]{:S(2)}, u32[]{:S(2)}) %collective-permute-start.1) | collective-permute-done | bytes 262176 | tf_op jit(solution)/shard_map/while/body/eval_jaxpr/ppermute | solution.py:15
  641.9 3.1 collective-permute-start.2
  645.0 6.0 collective-permute-done.2
  653.5 7.2 %collective-permute-done.3 = bf16[32,4096]{1,0:T(8,128)(2,1)S(1)} collective-permute-done((bf16[32,4096]{1,0:T(8,128)(2,1)S(1)}, bf16[32,4096]{1,0:T(8,128)(2,1)S(1)}, u32[]{:S(2)}, u32[]{:S(2)}) %collective-permute-start.3) | collective-permute-done | bytes 262176 | tf_op jit(solution)/shard_map/while/body/eval_jaxpr/ppermute | solution.py:21
  (60 shorter events, 20.4 us)
Async XLA Ops:
  6.5 0.8 copy-start
  7.4 86.3 %copy-start.1 = (bf16[4096,128]{1,0:T(8,128)(2,1)S(1)}, bf16[4096,128]{1,0:T(8,128)(2,1)}, u32[]{:S(2)}) copy-start(bf16[4096,128]{1,0:T(8,128)(2,1)} %get-tuple-element.378) | copy-start | bytes 3145732 | tf_op jit(solution)/shard_map/while
  7.4 86.3 %copy-start.2 = (bf16[128,4096]{1,0:T(8,128)(2,1)S(1)}, bf16[128,4096]{1,0:T(8,128)(2,1)}, u32[]{:S(2)}) copy-start(bf16[128,4096]{1,0:T(8,128)(2,1)} %get-tuple-element.379) | copy-start | bytes 3145732 | tf_op jit(solution)/shard_map/while
  7.4 82.5 %all-gather.2.cloned.1.call-start = ((), (), s32[]{:S(2)}) async-start(), calls=%async_computation.1 | async-start | bytes 4456448 | tf_op jit(solution)/shard_map/while/body/eval_jaxpr/all_gather | solution.py:52
  9.6 186.9 %reduce-scatter.2.cloned.1.call-start = ((), (), s32[]{:S(2)}) async-start(), calls=%async_computation.2 | async-start | bytes 4456448 | tf_op jit(solution)/shard_map/while/body/eval_jaxpr/reduce_scatter | solution.py:55
  196.6 1.7 collective-permute-start
  199.3 8.4 %collective-permute-start.1 = (bf16[32,4096]{1,0:T(8,128)(2,1)S(1)}, bf16[32,4096]{1,0:T(8,128)(2,1)S(1)}, u32[]{:S(2)}, u32[]{:S(2)}) collective-permute-start(bf16[32,4096]{1,0:T(8,128)(2,1)S(1)} %fusion.39), channel_id=1, source_target_pairs={{0,32},{16,48},{32,0},{48,16},{64,96},{80,112},{96,64},{112,80},{1... | collective-permute-start | bytes 786440 | tf_op jit(solution)/shard_map/while/body/eval_jaxpr/ppermute | solution.py:15
  208.8 9.1 %collective-permute-start.2 = (bf16[32,4096]{1,0:T(8,128)(2,1)S(1)}, bf16[32,4096]{1,0:T(8,128)(2,1)S(1)}, u32[]{:S(2)}, u32[]{:S(2)}) collective-permute-start(bf16[32,4096]{1,0:T(8,128)(2,1)S(1)} %fusion.40), channel_id=1, source_target_pairs={{0,64},{16,80},{32,96},{48,112},{64,0},{80,16},{96,32},{112,48},{1... | collective-permute-start | bytes 786440 | tf_op jit(solution)/shard_map/while/body/eval_jaxpr/ppermute | solution.py:15
  219.0 8.5 %collective-permute-start.3 = (bf16[32,4096]{1,0:T(8,128)(2,1)S(1)}, bf16[32,4096]{1,0:T(8,128)(2,1)S(1)}, u32[]{:S(2)}, u32[]{:S(2)}) collective-permute-start(bf16[32,4096]{1,0:T(8,128)(2,1)S(1)} %fusion.41), channel_id=1, source_target_pairs={{0,128},{16,144},{32,160},{48,176},{64,192},{80,208},{96,224},{112... | collective-permute-start | bytes 786440 | tf_op jit(solution)/shard_map/while/body/eval_jaxpr/ppermute | solution.py:21
  227.5 82.5 %copy-start.1 = (bf16[4096,128]{1,0:T(8,128)(2,1)S(1)}, bf16[4096,128]{1,0:T(8,128)(2,1)}, u32[]{:S(2)}) copy-start(bf16[4096,128]{1,0:T(8,128)(2,1)} %get-tuple-element.378) | copy-start | bytes 3145732 | tf_op jit(solution)/shard_map/while
  227.5 82.5 %copy-start.2 = (bf16[128,4096]{1,0:T(8,128)(2,1)S(1)}, bf16[128,4096]{1,0:T(8,128)(2,1)}, u32[]{:S(2)}) copy-start(bf16[128,4096]{1,0:T(8,128)(2,1)} %get-tuple-element.379) | copy-start | bytes 3145732 | tf_op jit(solution)/shard_map/while
  227.5 78.7 %all-gather.2.cloned.1.call-start = ((), (), s32[]{:S(2)}) async-start(), calls=%async_computation.1 | async-start | bytes 4456448 | tf_op jit(solution)/shard_map/while/body/eval_jaxpr/all_gather | solution.py:52
  229.7 183.3 %reduce-scatter.2.cloned.1.call-start = ((), (), s32[]{:S(2)}) async-start(), calls=%async_computation.2 | async-start | bytes 4456448 | tf_op jit(solution)/shard_map/while/body/eval_jaxpr/reduce_scatter | solution.py:55
  413.0 1.7 collective-permute-start
  415.8 8.4 %collective-permute-start.1 = (bf16[32,4096]{1,0:T(8,128)(2,1)S(1)}, bf16[32,4096]{1,0:T(8,128)(2,1)S(1)}, u32[]{:S(2)}, u32[]{:S(2)}) collective-permute-start(bf16[32,4096]{1,0:T(8,128)(2,1)S(1)} %fusion.39), channel_id=1, source_target_pairs={{0,32},{16,48},{32,0},{48,16},{64,96},{80,112},{96,64},{112,80},{1... | collective-permute-start | bytes 786440 | tf_op jit(solution)/shard_map/while/body/eval_jaxpr/ppermute | solution.py:15
  425.3 9.1 %collective-permute-start.2 = (bf16[32,4096]{1,0:T(8,128)(2,1)S(1)}, bf16[32,4096]{1,0:T(8,128)(2,1)S(1)}, u32[]{:S(2)}, u32[]{:S(2)}) collective-permute-start(bf16[32,4096]{1,0:T(8,128)(2,1)S(1)} %fusion.40), channel_id=1, source_target_pairs={{0,64},{16,80},{32,96},{48,112},{64,0},{80,16},{96,32},{112,48},{1... | collective-permute-start | bytes 786440 | tf_op jit(solution)/shard_map/while/body/eval_jaxpr/ppermute | solution.py:15
  435.5 8.5 %collective-permute-start.3 = (bf16[32,4096]{1,0:T(8,128)(2,1)S(1)}, bf16[32,4096]{1,0:T(8,128)(2,1)S(1)}, u32[]{:S(2)}, u32[]{:S(2)}) collective-permute-start(bf16[32,4096]{1,0:T(8,128)(2,1)S(1)} %fusion.41), channel_id=1, source_target_pairs={{0,128},{16,144},{32,160},{48,176},{64,192},{80,208},{96,224},{112... | collective-permute-start | bytes 786440 | tf_op jit(solution)/shard_map/while/body/eval_jaxpr/ppermute | solution.py:21
  444.0 82.2 %copy-start.1 = (bf16[4096,128]{1,0:T(8,128)(2,1)S(1)}, bf16[4096,128]{1,0:T(8,128)(2,1)}, u32[]{:S(2)}) copy-start(bf16[4096,128]{1,0:T(8,128)(2,1)} %get-tuple-element.378) | copy-start | bytes 3145732 | tf_op jit(solution)/shard_map/while
  444.0 82.2 %copy-start.2 = (bf16[128,4096]{1,0:T(8,128)(2,1)S(1)}, bf16[128,4096]{1,0:T(8,128)(2,1)}, u32[]{:S(2)}) copy-start(bf16[128,4096]{1,0:T(8,128)(2,1)} %get-tuple-element.379) | copy-start | bytes 3145732 | tf_op jit(solution)/shard_map/while
  444.0 78.5 %all-gather.2.cloned.1.call-start = ((), (), s32[]{:S(2)}) async-start(), calls=%async_computation.1 | async-start | bytes 4456448 | tf_op jit(solution)/shard_map/while/body/eval_jaxpr/all_gather | solution.py:52
  446.2 183.4 %reduce-scatter.2.cloned.1.call-start = ((), (), s32[]{:S(2)}) async-start(), calls=%async_computation.2 | async-start | bytes 4456448 | tf_op jit(solution)/shard_map/while/body/eval_jaxpr/reduce_scatter | solution.py:55
  629.7 1.7 collective-permute-start
  632.4 8.4 %collective-permute-start.1 = (bf16[32,4096]{1,0:T(8,128)(2,1)S(1)}, bf16[32,4096]{1,0:T(8,128)(2,1)S(1)}, u32[]{:S(2)}, u32[]{:S(2)}) collective-permute-start(bf16[32,4096]{1,0:T(8,128)(2,1)S(1)} %fusion.39), channel_id=1, source_target_pairs={{0,32},{16,48},{32,0},{48,16},{64,96},{80,112},{96,64},{112,80},{1... | collective-permute-start | bytes 786440 | tf_op jit(solution)/shard_map/while/body/eval_jaxpr/ppermute | solution.py:15
  641.9 9.1 %collective-permute-start.2 = (bf16[32,4096]{1,0:T(8,128)(2,1)S(1)}, bf16[32,4096]{1,0:T(8,128)(2,1)S(1)}, u32[]{:S(2)}, u32[]{:S(2)}) collective-permute-start(bf16[32,4096]{1,0:T(8,128)(2,1)S(1)} %fusion.40), channel_id=1, source_target_pairs={{0,64},{16,80},{32,96},{48,112},{64,0},{80,16},{96,32},{112,48},{1... | collective-permute-start | bytes 786440 | tf_op jit(solution)/shard_map/while/body/eval_jaxpr/ppermute | solution.py:15
  652.1 8.5 %collective-permute-start.3 = (bf16[32,4096]{1,0:T(8,128)(2,1)S(1)}, bf16[32,4096]{1,0:T(8,128)(2,1)S(1)}, u32[]{:S(2)}, u32[]{:S(2)}) collective-permute-start(bf16[32,4096]{1,0:T(8,128)(2,1)S(1)} %fusion.41), channel_id=1, source_target_pairs={{0,128},{16,144},{32,160},{48,176},{64,192},{80,208},{96,224},{112... | collective-permute-start | bytes 786440 | tf_op jit(solution)/shard_map/while/body/eval_jaxpr/ppermute | solution.py:21
  660.6 0.6 copy-start.3
Sparse Core Ops, SparseCore 0:
  10.6 79.2 all-gather.1
  102.5 94.0 reduce-scatter.1
  230.8 75.4 all-gather.1
  318.8 94.1 reduce-scatter.1
  446.9 75.4 all-gather.1
  535.0 94.5 reduce-scatter.1
where the time goes:
time: 669 us; the launch traced here: 668 us
  waiting for transfers between devices  582 us (87%)
  matrix products  37.1 us (6%)
  starting transfers between devices  17.9 us (3%)
  other arithmetic  16 us (2%)
  between operations  13.4 us (2%)
    reduce_scatter x3, waiting for transfers between devices, partial_sum(): lax.psum_scatter(row_terms.astype(jnp.bfloat16), 'tp', scatter_dimension=...  283 us
    all_gather x3, waiting for transfers between devices, partial_sum(): row_terms = project(lax.all_gather(normed, 'tp', axis=0, tiled=True))  233 us
    ppermute x9, waiting for transfers between devices, swapped(): return lax.ppermute(value, axis, pairs)  44 us
    dot_general x3, matrix products, project(): return jnp.dot(active, down_local, preferred_element_type=jnp.float32)  25.9 us
    ppermute x3, waiting for transfers between devices, shifted(): lax.ppermute(value, axis, [(source, source + steps) for source in range(l...  21.5 us
    ppermute x9, starting transfers between devices, swapped(): return lax.ppermute(value, axis, pairs)  13.8 us
  transfers between devices with their start and end apart: 18, of which 18 were waited for; matrix products, arithmetic and copies ran while one was open for 0% of the time, Pallas kernels for 0%

commit v1 on v0

v1 whole, which is shorter than its diff:
```python
import jax
import jax.numpy as jnp
from jax import lax
from jax.sharding import PartitionSpec as P

LAYERS = 2
PIECES = 1


epsilon = 1e-05


def swapped(value, axis, mask):
    pairs = [(source, source ^ mask) for source in range(lax.axis_size(axis))]
    return lax.ppermute(value, axis, pairs)


def shifted(value, axis, steps):
    count = lax.axis_size(axis)
    return lax.ppermute(value, axis, [(source, source + steps) for source in range(count - steps)])


def body(tokens, norm_gains, w_gate, w_up, w_down):
    section_count = lax.axis_size("section")
    split = section_count // LAYERS
    bit_count = split.bit_length() - 1
    position = lax.axis_index("section")
    section_layer = position // split
    member = position % split
    core = member % 2
    xpos = member // 2
    x_count = split // 2

    micro_count, tok_dev, model_width = tokens.shape
    piece_width = model_width // split
    half_width = model_width // 2
    row_count = tok_dev // PIECES
    piece_count = micro_count * PIECES
    tick_count = piece_count + LAYERS - 1

    def pick(value, axis, which):
        shape = value.shape
        grouped = value.reshape(shape[:axis] + (x_count, 2, piece_width) + shape[axis + 1:])
        chosen = lax.dynamic_index_in_dim(grouped, which, axis + 1, keepdims=False)
        return chosen.reshape(shape[:axis] + (half_width,) + shape[axis + 1:])

    other = 1 - core
    gate_own = pick(w_gate[0], 0, core)
    gate_other = pick(w_gate[0], 0, other)
    up_own = pick(w_up[0], 0, core)
    up_other = pick(w_up[0], 0, other)
    down_own = pick(w_down[0], 1, core)
    down_other = pick(w_down[0], 1, other)
    norm_gain = lax.dynamic_index_in_dim(norm_gains, section_layer, 0, keepdims=False)
    gain_own = pick(norm_gain, 0, core)

    def from_tokens(piece_index):
        micro_index, part = divmod(piece_index, PIECES)
        rows = tokens[micro_index, part * row_count:(part + 1) * row_count].astype(jnp.float32)
        return pick(rows, 1, core), jnp.sum(rows * rows, axis=1, keepdims=True)

    def from_received(received):
        current = received.astype(jnp.float32)
        own_sq = jnp.sum(current * current, axis=1, keepdims=True)
        return current, own_sq + swapped(own_sq, "section", 1)

    def tick(current, square_sum):
        inv_rms = lax.rsqrt(square_sum / model_width + epsilon)
        normed = (current * inv_rms * gain_own).astype(jnp.bfloat16)
        gathered = lax.all_gather(normed, "tp", axis=0, tiled=True)
        gathered_other = swapped(gathered, "section", 1)
        gate_proj = jnp.dot(gathered, gate_own, preferred_element_type=jnp.float32) + jnp.dot(
            gathered_other, gate_other, preferred_element_type=jnp.float32
        )
        up_proj = jnp.dot(gathered, up_own, preferred_element_type=jnp.float32) + jnp.dot(
            gathered_other, up_other, preferred_element_type=jnp.float32
        )
        active = (jax.nn.silu(gate_proj) * up_proj).astype(jnp.bfloat16)
        part_other = jnp.dot(active, down_other, preferred_element_type=jnp.float32).astype(jnp.bfloat16)
        part_from_other = swapped(part_other, "section", 1)
        part_own = jnp.dot(active, down_own, preferred_element_type=jnp.float32).astype(jnp.bfloat16)
        pair = (part_own.astype(jnp.float32) + part_from_other.astype(jnp.float32)).astype(jnp.bfloat16)
        summed = lax.psum_scatter(pair, "tp", scatter_dimension=0, tiled=True)
        for level in range(1, bit_count):
            summed = (
                summed.astype(jnp.float32) + swapped(summed, "section", 1 << level).astype(jnp.float32)
            )
            if level < bit_count - 1:
                summed = summed.astype(jnp.bfloat16)
        full_half = (current + summed.astype(jnp.float32)).astype(jnp.bfloat16)
        block = lax.dynamic_index_in_dim(
            full_half.reshape(row_count, x_count, piece_width), xpos, 1, keepdims=False
        )
        return full_half, block

    blocks = []
    received = None
    for tick_index in range(tick_count):
        if tick_index == 0:
            current, square_sum = from_tokens(0)
        elif tick_index >= piece_count:
            current, square_sum = from_received(received)
        else:
            first_current, first_sum = from_tokens(tick_index)
            later_current, later_sum = from_received(received)
            is_first = section_layer == 0
            current = jnp.where(is_first, first_current, later_current)
            square_sum = jnp.where(is_first, first_sum, later_sum)
        full_half, block = tick(current, square_sum)
        blocks.append(block)
        if tick_index < tick_count - 1:
            received = shifted(full_half, "section", split)

    stacked = jnp.stack(blocks, axis=0)
    outputs = []
    for micro_index in range(micro_count):
        parts = [
            lax.dynamic_index_in_dim(stacked, micro_index * PIECES + part + section_layer, 0, keepdims=False)
            for part in range(PIECES)
        ]
        outputs.append(jnp.concatenate(parts, axis=0))
    return jnp.stack(outputs, axis=0)[None]


def solution(mesh):
    in_specs = (
        P(None, "tp", None),
        P(),
        P("section", None, "tp"),
        P("section", None, "tp"),
        P("section", "tp", None),
    )
    out_specs = P("section", None, "tp", None)
    return jax.shard_map(body, mesh=mesh, in_specs=in_specs, out_specs=out_specs, check_vma=False)
```

time: 669 us -> 559 us (0.84)
  waiting for transfers between devices: 582 us -> 486 us
  matrix products: 37.1 us -> 23.5 us
  other arithmetic: 16 us -> 8.52 us
    all_gather x3, waiting for transfers between devices: 233 us -> 174 us  [tick(): gathered = lax.all_gather(normed, 'tp', axis=0, tiled=True)]
    reduce_scatter x3, waiting for transfers between devices: 283 us -> 263 us  [tick(): summed = lax.psum_scatter(pair, 'tp', scatter_dimension=0, tiled=True)]
    dot_general x6 -> x18, matrix products: 37.1 us -> 23.5 us  [the longest x3 6.17 us: tick(): jnp.dot(active, down_own, preferred_element_type=jnp.float32)]
    ppermute x3 -> x2, waiting for transfers between devices: 21.5 us -> 11.1 us  [shifted(): lax.ppermute(value, axis, [(source, source + steps) for source in range(c...]
    ppermute x9 -> x14, waiting for transfers between devices: 44 us -> 37.7 us  [swapped(): return lax.ppermute(value, axis, pairs)]
    ppermute x9 -> x14, starting transfers between devices: 13.8 us -> 14.8 us  [swapped(): return lax.ppermute(value, axis, pairs)]
  transfers between devices with their start and end apart: 18 -> 22, of which waited for: 18 -> 21; matrix products, arithmetic and copies ran while one was open for 0% -> 2% of each run, Pallas kernels for 0% -> 0%
where the time goes in v1:
time: 559 us; the launch traced here: 557 us
  waiting for transfers between devices  486 us (87%)
  matrix products  23.5 us (4%)
  starting transfers between devices  17.6 us (3%)
  between operations  13.9 us (2%)
  other arithmetic  8.52 us (2%)
  local copies, waits for them, and re-layouts  7.12 us (1%)
    reduce_scatter x3, waiting for transfers between devices, tick(): summed = lax.psum_scatter(pair, 'tp', scatter_dimension=0, tiled=True)  263 us
    all_gather x3, waiting for transfers between devices, tick(): gathered = lax.all_gather(normed, 'tp', axis=0, tiled=True)  174 us
    ppermute x14, waiting for transfers between devices, swapped(): return lax.ppermute(value, axis, pairs)  37.7 us
    ppermute x14, starting transfers between devices, swapped(): return lax.ppermute(value, axis, pairs)  14.8 us
  transfers between devices with their start and end apart: 22, of which 21 were waited for; matrix products, arithmetic and copies ran while one was open for 2% of the time, Pallas kernels for 0%

profile of v1, /device:TPU:32, one launch (start us, length us, event | category | flops | bytes accessed | tf_op | source)
XLA Modules:
  0.0 556.7 jit_solution(12921306199294246905)
XLA Ops:
  9.8 1.6 dynamic-slice_reduce_fusion
  12.4 61.0 %all-gather.4.cloned.1.call-done = bf16[512,2048]{1,0:T(8,128)(2,1)} async-done(((bf16[32,2048]{1,0:T(8,128)(2,1)}), bf16[512,2048]{1,0:T(8,128)(2,1)}) %all-gather.4.cloned.1.call-update) | async-done | bytes 2097168 | tf_op jit(solution)/shard_map/all_gather | solution.py:70
  73.4 1.6 copy.14
  75.2 1.8 constant_dynamic-slice_fusion.7
  78.8 2.3 convolution_add_fusion.5
  81.1 2.3 fusion.3
  84.8 3.8 collective-permute-done.1
  88.6 2.1 add_convert_fusion.2
  90.7 87.7 %reduce-scatter.4.cloned.1.call-done = bf16[32,2048]{1,0:T(8,128)(2,1)} async-done(((bf16[512,2048]{1,0:T(8,128)(2,1)}), bf16[32,2048]{1,0:T(8,128)(2,1)}) %reduce-scatter.4.cloned.1.call-update) | async-done | bytes 131088 | tf_op jit(solution)/shard_map/reduce_scatter | solution.py:83
  178.3 1.5 collective-permute-start.2
  179.8 3.7 collective-permute-done.2
  184.5 3.1 collective-permute-start.3
  187.5 3.5 collective-permute-done.3
  192.4 5.6 collective-permute-done.4
  200.1 56.6 %all-gather.6.cloned.1.call-done = bf16[512,2048]{1,0:T(8,128)(2,1)} async-done(((bf16[32,2048]{1,0:T(8,128)(2,1)}), bf16[512,2048]{1,0:T(8,128)(2,1)}) %all-gather.6.cloned.1.call-update) | async-done | bytes 2097168 | tf_op jit(solution)/shard_map/all_gather | solution.py:70
  256.8 2.4 fusion.15
  263.5 4.0 collective-permute-done.7
  267.6 2.1 add_convert_fusion.1
  269.7 87.6 %reduce-scatter.6.cloned.1.call-done = bf16[32,2048]{1,0:T(8,128)(2,1)} async-done(((bf16[512,2048]{1,0:T(8,128)(2,1)}), bf16[32,2048]{1,0:T(8,128)(2,1)}) %reduce-scatter.6.cloned.1.call-update) | async-done | bytes 131088 | tf_op jit(solution)/shard_map/reduce_scatter | solution.py:83
  358.8 3.7 collective-permute-done.8
  363.5 3.0 collective-permute-start.9
  366.5 3.5 collective-permute-done.9
  371.4 5.6 collective-permute-done.10
  379.2 56.6 %all-gather.8.cloned.1.call-done = bf16[512,2048]{1,0:T(8,128)(2,1)} async-done(((bf16[32,2048]{1,0:T(8,128)(2,1)}), bf16[512,2048]{1,0:T(8,128)(2,1)}) %all-gather.8.cloned.1.call-update) | async-done | bytes 2097168 | tf_op jit(solution)/shard_map/all_gather | solution.py:70
  435.8 2.4 fusion.17
  442.5 4.0 collective-permute-done.13
  446.5 2.1 add_convert_fusion
  448.6 87.6 %reduce-scatter.8.cloned.1.call-done = bf16[32,2048]{1,0:T(8,128)(2,1)} async-done(((bf16[512,2048]{1,0:T(8,128)(2,1)}), bf16[32,2048]{1,0:T(8,128)(2,1)}) %reduce-scatter.8.cloned.1.call-update) | async-done | bytes 131088 | tf_op jit(solution)/shard_map/reduce_scatter | solution.py:83
  536.2 1.5 collective-permute-start.14
  537.8 3.6 collective-permute-done.14
  542.4 3.1 collective-permute-start.15
  545.7 3.2 collective-permute-done.15
  (89 shorter events, 28.6 us)
Async XLA Ops:
  6.5 4.9 copy-start
  6.5 66.9 %all-gather.4.cloned.1.call-start = ((), (), s32[]{:S(2)}) async-start(), calls=%async_computation.3 | async-start | bytes 2228224 | tf_op jit(solution)/shard_map/all_gather | solution.py:70
  12.4 166.0 %reduce-scatter.4.cloned.1.call-start = ((), (), s32[]{:S(2)}) async-start(), calls=%async_computation.4 | async-start | bytes 2228224 | tf_op jit(solution)/shard_map/reduce_scatter | solution.py:83
  73.4 5.4 collective-permute-start
  75.2 2.2 copy-start.1
  77.0 4.1 copy-start.4
  84.2 4.4 collective-permute-start.1
  90.6 166.1 %all-gather.6.cloned.1.call-start = ((), (), s32[]{:S(2)}) async-start(), calls=%async_computation.5 | async-start | bytes 2228224 | tf_op jit(solution)/shard_map/all_gather | solution.py:70
  178.3 5.2 collective-permute-start.2
  184.5 6.6 %collective-permute-start.3 = (bf16[32,2048]{1,0:T(8,128)(2,1)S(1)}, bf16[32,2048]{1,0:T(8,128)(2,1)S(1)}, u32[]{:S(2)}, u32[]{:S(2)}) collective-permute-start(bf16[32,2048]{1,0:T(8,128)(2,1)S(1)} %add_convert_fusion.7), channel_id=1, source_target_pairs={{0,64},{16,80},{32,96},{48,112},{64,0},{80,16},{96,32},{112,48},{1... | collective-permute-start | bytes 393224 | tf_op jit(solution)/shard_map/ppermute | solution.py:15
  191.1 6.9 %collective-permute-start.4 = (bf16[32,2048]{1,0:T(8,128)(2,1)S(1)}, bf16[32,2048]{1,0:T(8,128)(2,1)S(1)}, u32[]{:S(2)}, u32[]{:S(2)}) collective-permute-start(bf16[32,2048]{1,0:T(8,128)(2,1)S(1)} %add_convert_fusion.6), channel_id=1, source_target_pairs={{0,128},{16,144},{32,160},{48,176},{64,192},{80,208},{96,224},{112... | collective-permute-start | bytes 393224 | tf_op jit(solution)/shard_map/ppermute | solution.py:20
  198.1 1.2 collective-permute-start.5
  200.1 157.2 %reduce-scatter.6.cloned.1.call-start = ((), (), s32[]{:S(2)}) async-start(), calls=%async_computation.6 | async-start | bytes 2228224 | tf_op jit(solution)/shard_map/reduce_scatter | solution.py:83
  256.8 2.5 copy-start.3
  256.8 4.4 collective-permute-start.6
  260.0 1.9 copy-start.5
  263.3 4.2 collective-permute-start.7
  269.7 166.1 %all-gather.8.cloned.1.call-start = ((), (), s32[]{:S(2)}) async-start(), calls=%async_computation.7 | async-start | bytes 2228224 | tf_op jit(solution)/shard_map/all_gather | solution.py:70
  357.3 5.2 collective-permute-start.8
  363.5 6.6 %collective-permute-start.9 = (bf16[32,2048]{1,0:T(8,128)(2,1)S(1)}, bf16[32,2048]{1,0:T(8,128)(2,1)S(1)}, u32[]{:S(2)}, u32[]{:S(2)}) collective-permute-start(bf16[32,2048]{1,0:T(8,128)(2,1)S(1)} %add_convert_fusion.5), channel_id=1, source_target_pairs={{0,64},{16,80},{32,96},{48,112},{64,0},{80,16},{96,32},{112,48},{1... | collective-permute-start | bytes 393224 | tf_op jit(solution)/shard_map/ppermute | solution.py:15
  370.1 6.9 %collective-permute-start.10 = (bf16[32,2048]{1,0:T(8,128)(2,1)S(1)}, bf16[32,2048]{1,0:T(8,128)(2,1)S(1)}, u32[]{:S(2)}, u32[]{:S(2)}) collective-permute-start(bf16[32,2048]{1,0:T(8,128)(2,1)S(1)} %add_convert_fusion.4), channel_id=1, source_target_pairs={{0,128},{16,144},{32,160},{48,176},{64,192},{80,208},{96,224},{112... | collective-permute-start | bytes 393224 | tf_op jit(solution)/shard_map/ppermute | solution.py:20
  377.1 1.2 collective-permute-start.11
  379.1 157.1 %reduce-scatter.8.cloned.1.call-start = ((), (), s32[]{:S(2)}) async-start(), calls=%async_computation.8 | async-start | bytes 2228224 | tf_op jit(solution)/shard_map/reduce_scatter | solution.py:83
  435.8 2.5 copy-start.2
  435.8 4.4 collective-permute-start.12
  438.9 1.9 copy-start.6
  442.3 4.2 collective-permute-start.13
  536.2 5.2 collective-permute-start.14
  542.4 6.6 %collective-permute-start.15 = (bf16[32,2048]{1,0:T(8,128)(2,1)S(1)}, bf16[32,2048]{1,0:T(8,128)(2,1)S(1)}, u32[]{:S(2)}, u32[]{:S(2)}) collective-permute-start(bf16[32,2048]{1,0:T(8,128)(2,1)S(1)} %add_convert_fusion.3), channel_id=1, source_target_pairs={{0,64},{16,80},{32,96},{48,112},{64,0},{80,16},{96,32},{112,48},{1... | collective-permute-start | bytes 393224 | tf_op jit(solution)/shard_map/ppermute | solution.py:15
Sparse Core Ops, SparseCore 0:
  12.5 60.9 all-gather.3
  90.8 87.5 reduce-scatter.3
  200.2 56.5 all-gather.5
  269.8 87.5 reduce-scatter.5
  379.2 56.4 all-gather.7
  448.7 87.4 reduce-scatter.7
